TPU v7x, 128 devices: a whole 4x4x4 slice. The times are simulated.
128 devices in a mesh: req: 64 (over z, y, x_hi, core), tp: 2 (over x_lo).
Axes of the slice: x: 4 (x_hi: 2, x_lo: 2; x = x_hi * 2 + x_lo), y: 4, z: 4, core: 2. Of those that a mesh axis runs over, the one named last changes fastest.
Arguments:
- hidden_in: bfloat16 [131072, 1536], P(('req', 'tp')), may hold values from -30 to 30
- segment_ids: int32 [131072], P('req'), may hold values from 0 to 9, as said below
- page_owner: int32 [2048], P('req'), may hold values from 0 to 63, as said below
- norm_gain: bfloat16 [1536], replicated, may hold values from 0.099609375 to 1.8984375
- w_qkv: bfloat16 [1536, 1536], P(None, 'tp'), may hold values from -16 to 16
- w_out: bfloat16 [768, 1536], P('tp'), may hold values from -0.625 to 0.625
Outputs:
- hidden_out: bfloat16 [131072, 1536], P(('req', 'tp'))
- kv_cache: bfloat16 [2048, 4, 2, 6144], P('req', 'tp')
Inputs may be any that keep to these rules, and one draw needn't show every extreme that they name: `segment_ids`: within a group the numbers never fall. 0 marks the shared prefix, which comes first with 128 to 512 tokens; 1 to 8 mark the requests (a request may be empty); 9 marks padding at the end. At least three quarters of each group's tokens are not padding, and some group has none. `page_owner`: for each page number p, the 64 groups name 64 different owners for their page p. A group names one owner for at most 1 of its pages.
All inputs are finite; a program needn't handle non-finite values.
Results may differ from a plain program's by a relative error of at most 0.0095.
Values may be sent and summed in bfloat16 or wider, within the bound.
No kernel may reach another device: no remote copies, remote signals or barrier semaphores. Data moves between devices by JAX's collectives and lax.ppermute only.
A program may use at most 128 MiB of HBM per device.

v0:
```python
import math

import jax
import jax.numpy as jnp
from jax import lax
from jax.sharding import PartitionSpec as P

HEAD = 96
HEADS_Q = 8
HEADS_KV = 4
PAGE = 64
REQS = 8


rotary_base = 100000.0
norm_eps = 1e-05
masked_score = -1e30


def positions_of(segments):
    length = segments.shape[0]
    counter = jnp.arange(length, dtype=jnp.int32)
    previous = jnp.concatenate([segments[:1] - 1, segments[:-1]])
    starts = lax.cummax(jnp.where(segments != previous, counter, 0), axis=0)
    prefix_len = jnp.sum((segments == 0).astype(jnp.int32))
    return counter - starts + jnp.where(segments > 0, prefix_len, 0)


def rotary_tables(positions, width):
    half_width = width // 2
    exponent = jnp.arange(half_width, dtype=jnp.float32) * (2.0 / width)
    inverse = jnp.power(jnp.float32(rotary_base), -exponent)
    angles = positions.astype(jnp.float32)[:, None] * inverse[None, :]
    return (jnp.cos(angles), jnp.sin(angles))


def rotate(vectors, cosine, sine_table):
    half_width = vectors.shape[-1] // 2
    front_half = vectors[..., :half_width]
    second = vectors[..., half_width:]
    cosine = cosine[:, None, :]
    sine_table = sine_table[:, None, :]
    return jnp.concatenate(
        [front_half * cosine - second * sine_table, second * cosine + front_half * sine_table],
        axis=-1,
    )


def normalize(token_rows, gain_vector):
    values = token_rows.astype(jnp.float32)
    inverse_root = lax.rsqrt(jnp.mean(values * values, axis=-1, keepdims=True) + norm_eps)
    return (values * inverse_root * gain_vector.astype(jnp.float32)).astype(jnp.bfloat16)


def attend(queries, key_vectors, value_vectors, query_segments, key_segments, query_offset):
    query_count = queries.shape[0]
    query_heads = queries.shape[1]
    head_width = queries.shape[2]
    key_count = key_vectors.shape[0]
    key_heads = key_vectors.shape[1]
    group_ratio = query_heads // key_heads
    query_block = math.gcd(query_count, max(8, 1024 // query_heads))
    factor = head_width ** (-0.5)
    grouped = queries.reshape(
        query_count // query_block, query_block, key_heads, group_ratio, head_width
    )
    segment_blocks = query_segments.reshape(query_count // query_block, query_block)
    key_places = jnp.arange(key_count, dtype=jnp.int32)

    def one_block(inputs):
        block_queries, block_segments, block_number = inputs
        query_start = query_offset + block_number * query_block
        query_places = query_start + jnp.arange(query_block, dtype=jnp.int32)
        allowed = (key_places[None, :] <= query_places[:, None]) & (
            (key_segments[None, :] == block_segments[:, None]) | (key_segments[None, :] == 0)
        )
        raw_scores = (
            jnp.einsum(
                "qhgd,khd->hgqk", block_queries, key_vectors, preferred_element_type=jnp.float32
            )
            * factor
        )
        masked = jnp.where(allowed, raw_scores, masked_score)
        row_max = jnp.max(masked, axis=-1, keepdims=True)
        weights = jnp.where(allowed, jnp.exp(masked - row_max), 0.0)
        totals = jnp.sum(weights, axis=-1)
        mixed_sum = jnp.einsum(
            "hgqk,khd->qhgd",
            weights.astype(jnp.bfloat16),
            value_vectors,
            preferred_element_type=jnp.float32,
        )
        result = mixed_sum / jnp.transpose(totals, (2, 0, 1))[..., None]
        return result.astype(jnp.bfloat16).reshape(query_block, query_heads * head_width)

    numbers = jnp.arange(query_count // query_block, dtype=jnp.int32)
    outputs = lax.map(one_block, (grouped, segment_blocks, numbers))
    return outputs.reshape(query_count, query_heads * head_width)


def shards(hidden_in, segment_ids, page_owner, norm_gain, w_qkv, w_out):
    tp_count = lax.axis_size("tp")
    req_count = lax.axis_size("req")
    group_len = segment_ids.shape[0]
    local_query = HEADS_Q // tp_count
    local_kv = HEADS_KV // tp_count
    query_width = local_query * HEAD
    kv_width = local_kv * HEAD
    positions = positions_of(segment_ids)
    cosine, sine_table = rotary_tables(positions, HEAD)
    normed_own = normalize(hidden_in, norm_gain)
    normed_all = lax.all_gather(normed_own, "tp", axis=0, tiled=True)
    projected = jnp.dot(normed_all, w_qkv, preferred_element_type=jnp.float32)
    queries = rotate(
        projected[:, :query_width].reshape(group_len, local_query, HEAD), cosine, sine_table
    ).astype(jnp.bfloat16)
    keys_local = rotate(
        projected[:, query_width : query_width + kv_width].reshape(group_len, local_kv, HEAD),
        cosine,
        sine_table,
    ).astype(jnp.bfloat16)
    values_local = (
        projected[:, query_width + kv_width :]
        .reshape(group_len, local_kv, HEAD)
        .astype(jnp.bfloat16)
    )
    attended = attend(queries, keys_local, values_local, segment_ids, segment_ids, 0)
    projected_out = lax.psum_scatter(
        jnp.dot(attended, w_out, preferred_element_type=jnp.float32).astype(jnp.bfloat16),
        "tp",
        scatter_dimension=0,
        tiled=True,
    ).astype(jnp.float32)
    hidden_out = (hidden_in.astype(jnp.float32) + projected_out).astype(jnp.bfloat16)
    page_count = group_len // PAGE
    lane_count = -(-page_count // req_count)
    key_pages = (
        keys_local.reshape(page_count, PAGE, local_kv, HEAD)
        .transpose(0, 2, 1, 3)
        .reshape(page_count, local_kv, PAGE * HEAD)
    )
    value_pages = (
        values_local.reshape(page_count, PAGE, local_kv, HEAD)
        .transpose(0, 2, 1, 3)
        .reshape(page_count, local_kv, PAGE * HEAD)
    )
    page_data = jnp.stack([key_pages, value_pages], axis=2).reshape(
        page_count, local_kv * 2 * PAGE * HEAD
    )
    live_pages = segment_ids[::PAGE] != REQS + 1
    page_numbers = jnp.arange(page_count, dtype=jnp.int32)
    same_owner = (
        (page_owner[:, None] == page_owner[None, :])
        & live_pages[None, :]
        & (page_numbers[None, :] < page_numbers[:, None])
    )
    page_rank = jnp.sum(same_owner.astype(jnp.int32), axis=1)
    owner_ids = jnp.arange(req_count, dtype=jnp.int32)
    lane_ids = jnp.arange(lane_count, dtype=jnp.int32)
    selection = (
        (page_owner[None, None, :] == owner_ids[:, None, None])
        & (page_rank[None, None, :] == lane_ids[None, :, None])
        & live_pages[None, None, :]
    )
    send_pages = jnp.einsum(
        "olp,pc->olc", selection.astype(jnp.bfloat16), page_data, preferred_element_type=jnp.float32
    ).astype(jnp.bfloat16)
    send_ids = jnp.sum(jnp.where(selection, page_numbers[None, None, :] + 1, 0), axis=2) - 1
    received, received_ids = (
        lax.all_to_all(send_pages, "req", split_axis=0, concat_axis=0, tiled=True),
        lax.all_to_all(send_ids, "req", split_axis=0, concat_axis=0, tiled=True),
    )
    placing = (
        received_ids.reshape(req_count * lane_count)[None, :] == page_numbers[:, None]
    ).astype(jnp.bfloat16)
    cache_rows = jnp.dot(
        placing,
        received.reshape(req_count * lane_count, local_kv * 2 * PAGE * HEAD),
        preferred_element_type=jnp.float32,
    ).astype(jnp.bfloat16)
    return (hidden_out, cache_rows.reshape(page_count, local_kv, 2, PAGE * HEAD))


def solution(mesh):
    placed = (P(("req", "tp"), None), P("req"), P("req"), P(), P(None, "tp"), P("tp", None))
    return jax.shard_map(
        shards,
        mesh=mesh,
        in_specs=placed,
        out_specs=(P(("req", "tp"), None), P("req", "tp", None, None)),
        check_vma=False,
    )
```

profile of v0, /device:TPU:1, one launch (start us, length us, event | category | flops | bytes accessed | tf_op | source)
XLA Modules:
  0.0 386.5 jit_solution(12783375643115999574)
XLA Ops:
  7.2 2.7 fusion.48
  10.2 2.4 fusion.50
  16.2 1.4 multiply_cosine_fusion
  17.7 81.0 %all-gather.2.cloned.1.call-done = bf16[2048,1536]{1,0:T(8,128)(2,1)} async-done(((bf16[1024,1536]{1,0:T(8,128)(2,1)}), bf16[2048,1536]{1,0:T(8,128)(2,1)}) %all-gather.2.cloned.1.call-update) | async-done | bytes 6291472 | tf_op jit(solution)/shard_map/all_gather | solution.py:112
  98.7 7.4 %fusion.76 = f32[2048,768]{0,1:T(8,128)S(1)} fusion(bf16[2048,1536]{1,0:T(8,128)(2,1)} %all-gather.2.cloned.1.call-done, bf16[1536,768]{1,0:T(8,128)(2,1)S(1)} %copy-done), kind=kOutput, calls=%fused_computation.89 | convolution fusion | flops 4831838208 | bytes 14942208 | tf_op jit(solution)/shard_map/dot_general | solution.py:113
  106.3 2.5 copy-done.3
  108.8 1.0 slice.68
  110.0 1.8 slice-done
  112.9 1.5 copy.39
  114.4 106.3 %while.11 = (s32[]{:T(128)}, bf16[8,256,384]{2,1,0:T(8,128)(2,1)}, s32[8]{0:T(128)S(1)}, s32[2048]{0:T(1024)S(1)}, s32[8,256]{1,0:T(8,128)S(1)}, /*index=5*/bf16...) while((s32[]{:T(128)}, bf16[8,256,384]{2,1,0:T(8,128)(2,1)}, ...), condition=%wide.region_7.8_spmd.clone, body=%wide.region_4.7_spmd.clone.sunk | while | flops 820187392 | bytes 12748933 | solution.py:97
  116.6 6.7 %fusion.95 = (f32[2,2,256]{2,1,0:T(2,128)S(1)}, bf16[2,2,256,2048]{3,2,1,0:T(8,128)(2,1)}) fusion(pred[256,2048]{1,0:T(8,128)(4,1)S(1)} %fusion.94, bf16[2048,2,96]{0,2,1:T(8,128)(2,1)S(1)} %get-tuple-element.215, bf16[8,256,2,2,96]{1,4,3,2,0:T(8,128)(2,1)} %get-tuple-element.214, s32[]{:T(128)} %get-tuple-element.199), kind=kOutput, calls=%fused_computation.88.clone.1 | convolution fusion | flops 415238144 | bytes 6230528 | tf_op jit(solution)/shard_map/while/body/eval_jaxpr/sub | solution.py:85
  123.3 3.6 fusion.96
  127.0 0.7 constant_dynamic-update-slice_fusion.2
  129.8 6.7 %fusion.95 = (f32[2,2,256]{2,1,0:T(2,128)S(1)}, bf16[2,2,256,2048]{3,2,1,0:T(8,128)(2,1)}) fusion(pred[256,2048]{1,0:T(8,128)(4,1)S(1)} %fusion.94, bf16[2048,2,96]{0,2,1:T(8,128)(2,1)S(1)} %get-tuple-element.215, bf16[8,256,2,2,96]{1,4,3,2,0:T(8,128)(2,1)} %get-tuple-element.214, s32[]{:T(128)} %get-tuple-element.199), kind=kOutput, calls=%fused_computation.88.clone.1 | convolution fusion | flops 415238144 | bytes 6230528 | tf_op jit(solution)/shard_map/while/body/eval_jaxpr/sub | solution.py:85
  136.5 3.6 fusion.96
  140.3 0.7 constant_dynamic-update-slice_fusion.2
  143.1 6.7 %fusion.95 = (f32[2,2,256]{2,1,0:T(2,128)S(1)}, bf16[2,2,256,2048]{3,2,1,0:T(8,128)(2,1)}) fusion(pred[256,2048]{1,0:T(8,128)(4,1)S(1)} %fusion.94, bf16[2048,2,96]{0,2,1:T(8,128)(2,1)S(1)} %get-tuple-element.215, bf16[8,256,2,2,96]{1,4,3,2,0:T(8,128)(2,1)} %get-tuple-element.214, s32[]{:T(128)} %get-tuple-element.199), kind=kOutput, calls=%fused_computation.88.clone.1 | convolution fusion | flops 415238144 | bytes 6230528 | tf_op jit(solution)/shard_map/while/body/eval_jaxpr/sub | solution.py:85
  149.8 3.6 fusion.96
  153.6 0.7 constant_dynamic-update-slice_fusion.2
  156.4 6.7 %fusion.95 = (f32[2,2,256]{2,1,0:T(2,128)S(1)}, bf16[2,2,256,2048]{3,2,1,0:T(8,128)(2,1)}) fusion(pred[256,2048]{1,0:T(8,128)(4,1)S(1)} %fusion.94, bf16[2048,2,96]{0,2,1:T(8,128)(2,1)S(1)} %get-tuple-element.215, bf16[8,256,2,2,96]{1,4,3,2,0:T(8,128)(2,1)} %get-tuple-element.214, s32[]{:T(128)} %get-tuple-element.199), kind=kOutput, calls=%fused_computation.88.clone.1 | convolution fusion | flops 415238144 | bytes 6230528 | tf_op jit(solution)/shard_map/while/body/eval_jaxpr/sub | solution.py:85
  163.1 3.6 fusion.96
  166.9 0.7 constant_dynamic-update-slice_fusion.2
  169.7 6.7 %fusion.95 = (f32[2,2,256]{2,1,0:T(2,128)S(1)}, bf16[2,2,256,2048]{3,2,1,0:T(8,128)(2,1)}) fusion(pred[256,2048]{1,0:T(8,128)(4,1)S(1)} %fusion.94, bf16[2048,2,96]{0,2,1:T(8,128)(2,1)S(1)} %get-tuple-element.215, bf16[8,256,2,2,96]{1,4,3,2,0:T(8,128)(2,1)} %get-tuple-element.214, s32[]{:T(128)} %get-tuple-element.199), kind=kOutput, calls=%fused_computation.88.clone.1 | convolution fusion | flops 415238144 | bytes 6230528 | tf_op jit(solution)/shard_map/while/body/eval_jaxpr/sub | solution.py:85
  176.4 3.6 fusion.96
  180.2 0.7 constant_dynamic-update-slice_fusion.2
  183.0 6.7 %fusion.95 = (f32[2,2,256]{2,1,0:T(2,128)S(1)}, bf16[2,2,256,2048]{3,2,1,0:T(8,128)(2,1)}) fusion(pred[256,2048]{1,0:T(8,128)(4,1)S(1)} %fusion.94, bf16[2048,2,96]{0,2,1:T(8,128)(2,1)S(1)} %get-tuple-element.215, bf16[8,256,2,2,96]{1,4,3,2,0:T(8,128)(2,1)} %get-tuple-element.214, s32[]{:T(128)} %get-tuple-element.199), kind=kOutput, calls=%fused_computation.88.clone.1 | convolution fusion | flops 415238144 | bytes 6230528 | tf_op jit(solution)/shard_map/while/body/eval_jaxpr/sub | solution.py:85
  189.7 3.6 fusion.96
  196.2 6.7 %fusion.95 = (f32[2,2,256]{2,1,0:T(2,128)S(1)}, bf16[2,2,256,2048]{3,2,1,0:T(8,128)(2,1)}) fusion(pred[256,2048]{1,0:T(8,128)(4,1)S(1)} %fusion.94, bf16[2048,2,96]{0,2,1:T(8,128)(2,1)S(1)} %get-tuple-element.215, bf16[8,256,2,2,96]{1,4,3,2,0:T(8,128)(2,1)} %get-tuple-element.214, s32[]{:T(128)} %get-tuple-element.199), kind=kOutput, calls=%fused_computation.88.clone.1 | convolution fusion | flops 415238144 | bytes 6230528 | tf_op jit(solution)/shard_map/while/body/eval_jaxpr/sub | solution.py:85
  202.9 3.6 fusion.96
  209.5 6.7 %fusion.95 = (f32[2,2,256]{2,1,0:T(2,128)S(1)}, bf16[2,2,256,2048]{3,2,1,0:T(8,128)(2,1)}) fusion(pred[256,2048]{1,0:T(8,128)(4,1)S(1)} %fusion.94, bf16[2048,2,96]{0,2,1:T(8,128)(2,1)S(1)} %get-tuple-element.215, bf16[8,256,2,2,96]{1,4,3,2,0:T(8,128)(2,1)} %get-tuple-element.214, s32[]{:T(128)} %get-tuple-element.199), kind=kOutput, calls=%fused_computation.88.clone.1 | convolution fusion | flops 415238144 | bytes 6230528 | tf_op jit(solution)/shard_map/while/body/eval_jaxpr/sub | solution.py:85
  216.2 3.6 fusion.96
  220.7 7.8 %convolution_convert_fusion.2 = bf16[2048,1536]{1,0:T(8,128)(2,1)} fusion(bf16[2048,384]{1,0:T(8,128)(2,1)} %bitcast.141, bf16[384,1536]{1,0:T(8,128)(2,1)} %param.13), kind=kOutput, calls=%fused_computation.41 | convolution fusion | flops 2419064832 | bytes 9043968 | tf_op jit(solution)/shard_map/dot_general | solution.py:129
  230.2 10.4 %all-to-all-start = ((s32[64,1,1]{2,1,0:T(1,128)}), s32[64,1,1]{2,1,0:T(1,128)S(1)}, u32[]{:S(2)}, u32[]{:S(2)}) async-start(s32[64,1,1]{2,1,0:T(1,128)} %copy.41), calls=%async_computation.1 | async-start | bytes 65536 | tf_op jit(solution)/shard_map/all_to_all | solution.py:171
  241.6 2.2 copy.44
  244.4 2.3 stack_reshape.6
  247.6 1.4 stack_reshape.7
  249.2 2.8 copy.46
  251.9 2.4 reshape.351
  254.3 2.8 fusion.47
  257.6 5.9 %reduce.4 = bf16[64,24576]{1,0:T(8,128)(2,1)} reduce(bf16[64,1,24576]{2,0,1:T(8,128)(2,1)} %fusion.47, bf16[]{:T(256)} %broadcast.248), dimensions={1}, to_apply=%copy.47.reduce_sub_computation | reduce | bytes 6291458 | tf_op jit(solution)/shard_map/convert_element_type | solution.py:167
  263.5 5.2 %reshape.358 = bf16[64,2,12288]{2,1,0:T(2,128)(2,1)} reshape(bf16[64,24576]{1,0:T(8,128)(2,1)} %reduce.4) | data formatting | bytes 6291456
  268.7 10.6 %all-to-all-start.1 = ((bf16[64,2,12288]{2,1,0:T(2,128)(2,1)}), bf16[64,2,12288]{2,1,0:T(2,128)(2,1)}, u32[]{:S(2)}, u32[]{:S(2)}) async-start(bf16[64,2,12288]{2,1,0:T(2,128)(2,1)} %reshape.358), calls=%async_computation.2 | async-start | bytes 6291456 | tf_op jit(solution)/shard_map/all_to_all | solution.py:170
  279.4 1.2 reduce.2
  280.6 67.6 %all-to-all-done.1 = bf16[64,2,12288]{2,1,0:T(2,128)(2,1)} async-done(((bf16[64,2,12288]{2,1,0:T(2,128)(2,1)}), bf16[64,2,12288]{2,1,0:T(2,128)(2,1)}, u32[]{:S(2)}, u32[]{:S(2)}) %all-to-all-start.1) | async-done | bytes 3145760 | tf_op jit(solution)/shard_map/all_to_all | solution.py:170
  348.2 17.4 %reshape.359 = bf16[64,1,24576]{2,1,0:T(2,128)(2,1)} reshape(bf16[64,2,12288]{2,1,0:T(2,128)(2,1)} %all-to-all-done.1) | data formatting | bytes 6291456
  365.6 6.6 %convolution_convert_fusion.1 = bf16[32,24576]{1,0:T(8,128)(2,1)S(1)} fusion(bf16[64,1,24576]{2,1,0:T(2,128)(2,1)} %reshape.359, s32[64]{0:T(128)S(1)} %reduce.2), kind=kOutput, calls=%fused_computation.37 | convolution fusion | flops 101451776 | bytes 4718848 | tf_op jit(solution)/shard_map/dot_general | solution.py:176
  372.2 2.1 reshape.353
  374.2 5.5 %fusion.51 = bf16[1024,1536]{1,0:T(8,128)(2,1)} fusion(bf16[1024,1536]{1,0:T(8,128)(2,1)} %param.8, bf16[1024,1536]{1,0:T(8,128)(2,1)} %reduce-scatter.2.cloned.1.call-done), kind=kLoop, calls=%fused_computation.45 | loop fusion | flops 6291456 | bytes 9437184 | tf_op jit(solution)/shard_map/convert_element_type | solution.py:134
  (116 shorter events, 23.8 us)
Async XLA Ops:
  7.2 91.5 %copy-start = (bf16[1536,768]{1,0:T(8,128)(2,1)S(1)}, bf16[1536,768]{1,0:T(8,128)(2,1)}, u32[]{:S(2)}) copy-start(bf16[1536,768]{1,0:T(8,128)(2,1)} %param.12) | copy-start | bytes 7077892
  7.2 2.8 copy-start.11
  7.2 91.5 %all-gather.2.cloned.1.call-start = ((), (), s32[]{:S(2)}) async-start(), calls=%async_computation.3 | async-start | bytes 9437184 | tf_op jit(solution)/shard_map/all_gather | solution.py:112
  7.2 2.9 copy-start.2
  12.6 0.7 copy-start.9
  12.7 361.6 %reduce-scatter.2.cloned.1.call-start = ((), (), s32[]{:S(2)}) async-start(), calls=%async_computation.4 | async-start | bytes 9437184 | tf_op jit(solution)/shard_map/reduce_scatter | solution.py:128
  106.1 2.7 copy-start.3
  109.8 2.0 slice-start
  110.0 4.4 %copy-start.5 = (bf16[2048,2,48]{0,2,1:T(8,128)(2,1)}, bf16[2048,2,48]{0,2,1:T(8,128)(2,1)S(1)}, u32[]{:S(2)}) copy-start(bf16[2048,2,48]{0,2,1:T(8,128)(2,1)S(1)} %get-tuple-element.129) | copy-start | bytes 1179652
  112.8 1.6 copy-start.7
  228.5 0.7 copy-start.10
  228.5 12.5 %copy-start.6 = (bf16[2048,2,48]{0,2,1:T(8,128)(2,1)S(1)}, bf16[2048,2,48]{0,2,1:T(8,128)(2,1)}, u32[]{:S(2)}) copy-start(bf16[2048,2,48]{0,2,1:T(8,128)(2,1)} %copy-done.5) | copy-start | bytes 1179652
  230.2 38.5 %all-to-all-start = ((s32[64,1,1]{2,1,0:T(1,128)}), s32[64,1,1]{2,1,0:T(1,128)S(1)}, u32[]{:S(2)}, u32[]{:S(2)}) async-start(s32[64,1,1]{2,1,0:T(1,128)} %copy.41), calls=%async_computation.1 | async-start | bytes 65536 | tf_op jit(solution)/shard_map/all_to_all | solution.py:171
  244.4 2.3 copy-start.4
  247.3 1.7 copy-start.8
  268.7 79.4 %all-to-all-start.1 = ((bf16[64,2,12288]{2,1,0:T(2,128)(2,1)}), bf16[64,2,12288]{2,1,0:T(2,128)(2,1)}, u32[]{:S(2)}, u32[]{:S(2)}) async-start(bf16[64,2,12288]{2,1,0:T(2,128)(2,1)} %reshape.358), calls=%async_computation.2 | async-start | bytes 6291456 | tf_op jit(solution)/shard_map/all_to_all | solution.py:170
  374.2 5.5 %copy-start.1 = (bf16[1536,768]{1,0:T(8,128)(2,1)S(1)}, bf16[1536,768]{1,0:T(8,128)(2,1)}, u32[]{:S(2)}) copy-start(bf16[1536,768]{1,0:T(8,128)(2,1)} %param.12) | copy-start | bytes 7077892
Sparse Core Ops, SparseCore 0:
  12.8 85.8 all-gather.1
  228.7 108.4 reduce-scatter.1
where the time goes:
time: 388 us; the launch traced here: 387 us
  waiting for transfers between devices  149 us (38%)
  matrix products  107 us (28%)
  local copies, waits for them, and re-layouts  60.6 us (16%)
  other arithmetic  28.4 us (7%)
  starting transfers between devices  21.1 us (5%)
  between operations  14.9 us (4%)
  loops' own time  5.93 us (2%)
    all_gather x1, waiting for transfers between devices, shards(): normed_all = lax.all_gather(normed_own, 'tp', axis=0, tiled=True)  81 us
    all_to_all x1, waiting for transfers between devices, shards(): lax.all_to_all(send_pages, 'req', split_axis=0, concat_axis=0, tiled=True)  67.6 us
    sub x8, matrix products, one_block(): weights = jnp.where(allowed, jnp.exp(masked - row_max), 0.0)  53.6 us
    dot_general x8, matrix products, one_block(): jnp.einsum('hgqk,khd->qhgd', weights.astype(jnp.bfloat16), value_vectors,...  28.8 us
    unnamed x29, local copies, waits for them, and re-layouts  28.4 us
    all_to_all x1, starting transfers between devices, shards(): lax.all_to_all(send_pages, 'req', split_axis=0, concat_axis=0, tiled=True)  10.6 us
    all_to_all x1, starting transfers between devices, shards(): lax.all_to_all(send_ids, 'req', split_axis=0, concat_axis=0, tiled=True)  10.4 us
    dot_general x1, matrix products, shards(): jnp.dot(attended, w_out, preferred_element_type=jnp.float32)  7.84 us
  transfers between devices with their start and end apart: 4, of which 2 were waited for; matrix products, arithmetic and copies ran while one was open for 16% of the time, Pallas kernels for 0%

commit v1 on v0

--- a/solution.py
+++ b/solution.py
@@ -101,16 +101,29 @@
 def shards(hidden_in, segment_ids, page_owner, norm_gain, w_qkv, w_out):
     tp_count = lax.axis_size("tp")
     req_count = lax.axis_size("req")
+    tp_index = lax.axis_index("tp")
+    req_index = lax.axis_index("req")
     group_len = segment_ids.shape[0]
+    half_len = hidden_in.shape[0]
     local_query = HEADS_Q // tp_count
     local_kv = HEADS_KV // tp_count
     query_width = local_query * HEAD
     kv_width = local_kv * HEAD
+    swap = [(0, 1), (1, 0)]
+    page_count = group_len // PAGE
+    live_pages = segment_ids[::PAGE] != REQS + 1
+    owner_code = jnp.where(live_pages, page_owner, -1)
+    owner_all = lax.all_gather(owner_code, "req", axis=0, tiled=False)
     positions = positions_of(segment_ids)
     cosine, sine_table = rotary_tables(positions, HEAD)
     normed_own = normalize(hidden_in, norm_gain)
-    normed_all = lax.all_gather(normed_own, "tp", axis=0, tiled=True)
-    projected = jnp.dot(normed_all, w_qkv, preferred_element_type=jnp.float32)
+    normed_other = lax.ppermute(normed_own, "tp", swap)
+    proj_own = jnp.dot(normed_own, w_qkv, preferred_element_type=jnp.float32)
+    proj_other = jnp.dot(normed_other, w_qkv, preferred_element_type=jnp.float32)
+    first = tp_index == 0
+    projected = jnp.concatenate(
+        [jnp.where(first, proj_own, proj_other), jnp.where(first, proj_other, proj_own)], axis=0
+    )
     queries = rotate(
         projected[:, :query_width].reshape(group_len, local_query, HEAD), cosine, sine_table
     ).astype(jnp.bfloat16)
@@ -124,59 +137,37 @@
         .reshape(group_len, local_kv, HEAD)
         .astype(jnp.bfloat16)
     )
-    attended = attend(queries, keys_local, values_local, segment_ids, segment_ids, 0)
-    projected_out = lax.psum_scatter(
-        jnp.dot(attended, w_out, preferred_element_type=jnp.float32).astype(jnp.bfloat16),
-        "tp",
-        scatter_dimension=0,
-        tiled=True,
-    ).astype(jnp.float32)
-    hidden_out = (hidden_in.astype(jnp.float32) + projected_out).astype(jnp.bfloat16)
-    page_count = group_len // PAGE
-    lane_count = -(-page_count // req_count)
-    key_pages = (
-        keys_local.reshape(page_count, PAGE, local_kv, HEAD)
-        .transpose(0, 2, 1, 3)
-        .reshape(page_count, local_kv, PAGE * HEAD)
-    )
-    value_pages = (
-        values_local.reshape(page_count, PAGE, local_kv, HEAD)
-        .transpose(0, 2, 1, 3)
-        .reshape(page_count, local_kv, PAGE * HEAD)
-    )
+    key_pages = keys_local.reshape(page_count, PAGE, local_kv, HEAD).transpose(0, 2, 1, 3)
+    value_pages = values_local.reshape(page_count, PAGE, local_kv, HEAD).transpose(0, 2, 1, 3)
     page_data = jnp.stack([key_pages, value_pages], axis=2).reshape(
         page_count, local_kv * 2 * PAGE * HEAD
     )
-    live_pages = segment_ids[::PAGE] != REQS + 1
+    owner_ids = jnp.arange(req_count, dtype=jnp.int32)
+    to_owner = owner_code[None, :] == owner_ids[:, None]
+    send_index = jnp.argmax(to_owner, axis=1)
+    send_pages = jnp.where(
+        jnp.any(to_owner, axis=1)[:, None], jnp.take(page_data, send_index, axis=0), 0
+    ).astype(jnp.bfloat16)
+    received = lax.all_to_all(send_pages, "req", split_axis=0, concat_axis=0, tiled=True)
     page_numbers = jnp.arange(page_count, dtype=jnp.int32)
-    same_owner = (
-        (page_owner[:, None] == page_owner[None, :])
-        & live_pages[None, :]
-        & (page_numbers[None, :] < page_numbers[:, None])
+    from_group = owner_all == req_index
+    from_group = from_group.T
+    source_group = jnp.argmax(from_group, axis=1)
+    cache_rows = jnp.where(
+        jnp.any(from_group, axis=1)[:, None], jnp.take(received, source_group, axis=0), 0
+    ).astype(jnp.bfloat16)
+    attended = attend(queries, keys_local, values_local, segment_ids, segment_ids, 0)
+    other_start = (1 - tp_index) * half_len
+    own_start = tp_index * half_len
+    attended_other = lax.dynamic_slice_in_dim(attended, other_start, half_len, axis=0)
+    attended_own = lax.dynamic_slice_in_dim(attended, own_start, half_len, axis=0)
+    partial_other = jnp.dot(attended_other, w_out, preferred_element_type=jnp.float32).astype(
+        jnp.bfloat16
     )
-    page_rank = jnp.sum(same_owner.astype(jnp.int32), axis=1)
-    owner_ids = jnp.arange(req_count, dtype=jnp.int32)
-    lane_ids = jnp.arange(lane_count, dtype=jnp.int32)
-    selection = (
-        (page_owner[None, None, :] == owner_ids[:, None, None])
-        & (page_rank[None, None, :] == lane_ids[None, :, None])
-        & live_pages[None, None, :]
-    )
-    send_pages = jnp.einsum(
-        "olp,pc->olc", selection.astype(jnp.bfloat16), page_data, preferred_element_type=jnp.float32
-    ).astype(jnp.bfloat16)
-    send_ids = jnp.sum(jnp.where(selection, page_numbers[None, None, :] + 1, 0), axis=2) - 1
-    received, received_ids = (
-        lax.all_to_all(send_pages, "req", split_axis=0, concat_axis=0, tiled=True),
-        lax.all_to_all(send_ids, "req", split_axis=0, concat_axis=0, tiled=True),
-    )
-    placing = (
-        received_ids.reshape(req_count * lane_count)[None, :] == page_numbers[:, None]
-    ).astype(jnp.bfloat16)
-    cache_rows = jnp.dot(
-        placing,
-        received.reshape(req_count * lane_count, local_kv * 2 * PAGE * HEAD),
-        preferred_element_type=jnp.float32,
+    partial_in = lax.ppermute(partial_other, "tp", swap)
+    partial_own = jnp.dot(attended_own, w_out, preferred_element_type=jnp.float32)
+    hidden_out = (
+        hidden_in.astype(jnp.float32) + partial_own + partial_in.astype(jnp.float32)
     ).astype(jnp.bfloat16)
     return (hidden_out, cache_rows.reshape(page_count, local_kv, 2, PAGE * HEAD))
 

time: 388 us -> 401 us (1.034); the launches traced: 387 us -> 393 us
  waiting for transfers between devices: 149 us -> 52.6 us
  blocking collectives: 0 us -> 83.3 us
  other arithmetic: 28.4 us -> 49.6 us
  local copies, waits for them, and re-layouts: 60.6 us -> 80.8 us
  between operations: 14.9 us -> 2.56 us
  starting transfers between devices: 21.1 us -> 15.9 us
  matrix products: 107 us -> 102 us
    unnamed x0 -> x1, blocking collectives: none -> 83.3 us
    all_gather x1 -> x0, waiting for transfers between devices: 81 us -> none  [shards(): normed_all = lax.all_gather(normed_own, 'tp', axis=0, tiled=True)]
    all_to_all x1, waiting for transfers between devices: 67.6 us -> 0.01 us  [shards(): lax.all_to_all(send_pages, 'req', split_axis=0, concat_axis=0, tiled=True)]
    ppermute x0 -> x2, waiting for transfers between devices: none -> 52.6 us  [the longest x1 52.6 us: shards(): normed_other = lax.ppermute(normed_own, 'tp', swap)]
    select_n x0 -> x5, other arithmetic: none -> 13.3 us  [the longest x2 9.01 us: shards(): jnp.where(jnp.any(to_owner, axis=1)[:, None], jnp.take(page_data, send_in...]
    all_to_all x1 -> x0, starting transfers between devices: 10.4 us -> none  [shards(): lax.all_to_all(send_ids, 'req', split_axis=0, concat_axis=0, tiled=True)]
    gather x0 -> x3, local copies, waits for them, and re-layouts: none -> 10.3 us  [the longest x2 5.9 us: shards(): jnp.take(received, source_group, axis=0)]
    convert_element_type x2 -> x1, other arithmetic: 11.3 us -> 1.33 us  [shards(): values_local = projected[:, query_width + kv_width:].reshape(group_len, l...]
  transfers between devices with their start and end apart: 4 -> 3, of which waited for: 2 -> 1; matrix products, arithmetic and copies ran while one was open for 16% -> 40% of each run, Pallas kernels for 0% -> 0%
where the time goes in v1:
time: 401 us; the launch traced here: 393 us
  matrix products  102 us (25%)
  blocking collectives  83.3 us (21%)
  local copies, waits for them, and re-layouts  80.8 us (20%)
  waiting for transfers between devices  52.6 us (13%)
  other arithmetic  49.6 us (12%)
  starting transfers between devices  15.9 us (4%)
  loops' own time  5.47 us (1%)
    unnamed x1, blocking collectives  83.3 us
    sub x8, matrix products, one_block(): weights = jnp.where(allowed, jnp.exp(masked - row_max), 0.0)  53.5 us
    ppermute x1, waiting for transfers between devices, shards(): normed_other = lax.ppermute(normed_own, 'tp', swap)  52.6 us
    unnamed x39, local copies, waits for them, and re-layouts  29.8 us
    dot_general x8, matrix products, one_block(): jnp.einsum('hgqk,khd->qhgd', weights.astype(jnp.bfloat16), value_vectors,...  28.9 us
    all_to_all x1, starting transfers between devices, shards(): lax.all_to_all(send_pages, 'req', split_axis=0, concat_axis=0, tiled=True)  13.6 us
    dynamic_slice x16, local copies, waits for them, and re-layouts, attend(): outputs = lax.map(one_block, (grouped, segment_blocks, numbers))  10.3 us
    select_n x2, other arithmetic, shards(): jnp.where(jnp.any(to_owner, axis=1)[:, None], jnp.take(page_data, send_in...  9.01 us
  transfers between devices with their start and end apart: 3, of which 1 were waited for; matrix products, arithmetic and copies ran while one was open for 40% of the time, Pallas kernels for 0%

profile of v1, /device:TPU:1, one launch (start us, length us, event | category | flops | bytes accessed | tf_op | source)
XLA Modules:
  0.0 392.6 jit_solution(8306479803850997446)
XLA Ops:
  1.5 2.8 fusion.47
  4.4 2.4 fusion.49
  6.8 2.0 collective-permute-start
  17.1 2.3 multiply_cosine_fusion
  19.5 4.5 %fusion.73 = f32[1024,768]{1,0:T(8,128)S(1)} fusion(bf16[1024,1536]{1,0:T(8,128)(2,1)} %fusion.49, bf16[1536,768]{1,0:T(8,128)(2,1)S(1)} %copy-done), kind=kOutput, calls=%fused_computation.98 | convolution fusion | flops 2415919104 | bytes 8650752 | tf_op jit(solution)/shard_map/dot_general | solution.py:121
  23.9 52.6 %collective-permute-done = bf16[1024,1536]{1,0:T(8,128)(2,1)} collective-permute-done((bf16[1024,1536]{1,0:T(8,128)(2,1)}, bf16[1024,1536]{1,0:T(8,128)(2,1)}, u32[]{:S(2)}, u32[]{:S(2)}) %collective-permute-start) | collective-permute-done | bytes 3145760 | tf_op jit(solution)/shard_map/ppermute | solution.py:120
  76.6 4.5 %broadcast_select_fusion.2 = (f32[1024,768]{1,0:T(8,128)S(1)}, f32[1024,768]{1,0:T(8,128)S(1)}) fusion(f32[1024,768]{1,0:T(8,128)S(1)} %fusion.73, pred[]{:T(512)S(6)} %eq.52, bf16[1024,1536]{1,0:T(8,128)(2,1)} %collective-permute-done, bf16[1536,768]{1,0:T(8,128)(2,1)S(1)} %copy-done), kind=kOutput, calls=%fused_computation.63 | convolution fusion | flops 2417491968 | bytes 14942209 | tf_op jit(solution)/shard_map/dot_general | solution.py:122
  84.1 2.2 copy.44
  86.3 2.5 convert_element_type.59
  88.7 2.8 copy.43
  91.5 2.6 subtract_convert_fusion.1
  94.0 3.6 copy.54
  99.5 2.0 copy.53
  101.5 2.4 copy.42
  103.9 2.4 subtract_convert_fusion
  108.5 3.0 maximum_bitcast_fusion
  111.5 3.5 pad_maximum_fusion.1
  116.9 4.2 %reshape.203 = bf16[32,24576]{1,0:T(8,128)(2,1)S(1)} reshape(bf16[32,2,2,64,96]{4,3,2,1,0:T(8,128)(2,1)} %copy.49) | data formatting | bytes 3145728 | tf_op jit(solution)/shard_map/reshape | solution.py:142
  121.2 4.4 %gather_fusion = bf16[64,24576]{1,0:T(8,128)(2,1)} fusion(bf16[32,24576]{1,0:T(8,128)(2,1)S(1)} %reshape.203, s32[1024]{0:T(1024)} %pad_clamp_fusion.1), kind=kCustom, calls=%fused_computation | custom fusion | bytes 6291712 | tf_op jit(solution)/shard_map/jit(_take)/gather | solution.py:149
  125.6 4.0 %fusion.53 = bf16[64,1,24576]{2,0,1:T(8,128)(2,1)} fusion(bf16[64,24576]{1,0:T(8,128)(2,1)} %gather_fusion, pred[64]{0:T(512)(128)(4,1)S(1)} %copy-done.13, pred[64]{0:T(512)(128)(4,1)S(1)} %copy-done.12), kind=kLoop, calls=%fused_computation.53 | loop fusion | flops 3145728 | bytes 6291584 | tf_op jit(solution)/shard_map/jit(_where)/select_n | solution.py:148
  130.1 5.0 %reduce.41 = bf16[64,24576]{1,0:T(8,128)(2,1)S(1)} reduce(bf16[64,1,24576]{2,0,1:T(8,128)(2,1)} %fusion.53, bf16[]{:T(256)} %broadcast.163), dimensions={1}, to_apply=%copy.50.reduce_sub_computation | reduce | bytes 6291458 | tf_op jit(solution)/shard_map/jit(_where)/select_n | solution.py:148
  135.2 3.6 reshape.233
  138.7 13.6 %all-to-all-start = ((bf16[64,2,12288]{2,1,0:T(2,128)(2,1)}), bf16[64,2,12288]{2,1,0:T(2,128)(2,1)}, u32[]{:S(2)}, u32[]{:S(2)}) async-start(bf16[64,2,12288]{2,1,0:T(2,128)(2,1)} %reshape.233), calls=%async_computation | async-start | bytes 6291456 | tf_op jit(solution)/shard_map/all_to_all | solution.py:151
  152.3 110.7 %while.11 = (s32[]{:T(128)}, bf16[8,256,384]{2,1,0:T(8,128)(2,1)}, s32[8]{0:T(128)S(1)}, s32[2048]{0:T(1024)S(1)}, s32[8,256]{1,0:T(8,128)}, /*index=5*/bf16[8,2...) while((s32[]{:T(128)}, bf16[8,256,384]{2,1,0:T(8,128)(2,1)}, ...), condition=%wide.region_7.8_spmd.clone, body=%wide.region_4.7_spmd.clone.sunk | while | flops 820187392 | bytes 12747925 | solution.py:97
  155.0 6.7 %fusion.93 = (f32[2,2,256]{2,1,0:T(2,128)S(1)}, bf16[2,2,256,2048]{3,2,1,0:T(8,128)(2,1)}) fusion(pred[256,2048]{1,0:T(8,128)(4,1)S(1)} %fusion.92, bf16[2048,2,96]{0,2,1:T(8,128)(2,1)S(1)} %get-tuple-element.223, bf16[8,256,2,2,96]{1,4,3,2,0:T(8,128)(2,1)} %get-tuple-element.222, s32[]{:T(128)S(6)} %copy.68), kind=kOutput, calls=%fused_computation.97.clone.1 | convolution fusion | flops 415238144 | bytes 6230020 | tf_op jit(solution)/shard_map/while/body/eval_jaxpr/sub | solution.py:85
  161.7 3.6 fusion.94
  168.9 6.7 %fusion.93 = (f32[2,2,256]{2,1,0:T(2,128)S(1)}, bf16[2,2,256,2048]{3,2,1,0:T(8,128)(2,1)}) fusion(pred[256,2048]{1,0:T(8,128)(4,1)S(1)} %fusion.92, bf16[2048,2,96]{0,2,1:T(8,128)(2,1)S(1)} %get-tuple-element.223, bf16[8,256,2,2,96]{1,4,3,2,0:T(8,128)(2,1)} %get-tuple-element.222, s32[]{:T(128)S(6)} %copy.68), kind=kOutput, calls=%fused_computation.97.clone.1 | convolution fusion | flops 415238144 | bytes 6230020 | tf_op jit(solution)/shard_map/while/body/eval_jaxpr/sub | solution.py:85
  175.6 3.6 fusion.94
  182.7 6.7 %fusion.93 = (f32[2,2,256]{2,1,0:T(2,128)S(1)}, bf16[2,2,256,2048]{3,2,1,0:T(8,128)(2,1)}) fusion(pred[256,2048]{1,0:T(8,128)(4,1)S(1)} %fusion.92, bf16[2048,2,96]{0,2,1:T(8,128)(2,1)S(1)} %get-tuple-element.223, bf16[8,256,2,2,96]{1,4,3,2,0:T(8,128)(2,1)} %get-tuple-element.222, s32[]{:T(128)S(6)} %copy.68), kind=kOutput, calls=%fused_computation.97.clone.1 | convolution fusion | flops 415238144 | bytes 6230020 | tf_op jit(solution)/shard_map/while/body/eval_jaxpr/sub | solution.py:85
  189.4 3.6 fusion.94
  196.5 6.7 %fusion.93 = (f32[2,2,256]{2,1,0:T(2,128)S(1)}, bf16[2,2,256,2048]{3,2,1,0:T(8,128)(2,1)}) fusion(pred[256,2048]{1,0:T(8,128)(4,1)S(1)} %fusion.92, bf16[2048,2,96]{0,2,1:T(8,128)(2,1)S(1)} %get-tuple-element.223, bf16[8,256,2,2,96]{1,4,3,2,0:T(8,128)(2,1)} %get-tuple-element.222, s32[]{:T(128)S(6)} %copy.68), kind=kOutput, calls=%fused_computation.97.clone.1 | convolution fusion | flops 415238144 | bytes 6230020 | tf_op jit(solution)/shard_map/while/body/eval_jaxpr/sub | solution.py:85
  203.2 3.6 fusion.94
  210.4 6.7 %fusion.93 = (f32[2,2,256]{2,1,0:T(2,128)S(1)}, bf16[2,2,256,2048]{3,2,1,0:T(8,128)(2,1)}) fusion(pred[256,2048]{1,0:T(8,128)(4,1)S(1)} %fusion.92, bf16[2048,2,96]{0,2,1:T(8,128)(2,1)S(1)} %get-tuple-element.223, bf16[8,256,2,2,96]{1,4,3,2,0:T(8,128)(2,1)} %get-tuple-element.222, s32[]{:T(128)S(6)} %copy.68), kind=kOutput, calls=%fused_computation.97.clone.1 | convolution fusion | flops 415238144 | bytes 6230020 | tf_op jit(solution)/shard_map/while/body/eval_jaxpr/sub | solution.py:85
  217.1 3.6 fusion.94
  224.2 6.7 %fusion.93 = (f32[2,2,256]{2,1,0:T(2,128)S(1)}, bf16[2,2,256,2048]{3,2,1,0:T(8,128)(2,1)}) fusion(pred[256,2048]{1,0:T(8,128)(4,1)S(1)} %fusion.92, bf16[2048,2,96]{0,2,1:T(8,128)(2,1)S(1)} %get-tuple-element.223, bf16[8,256,2,2,96]{1,4,3,2,0:T(8,128)(2,1)} %get-tuple-element.222, s32[]{:T(128)S(6)} %copy.68), kind=kOutput, calls=%fused_computation.97.clone.1 | convolution fusion | flops 415238144 | bytes 6230020 | tf_op jit(solution)/shard_map/while/body/eval_jaxpr/sub | solution.py:85
  230.9 3.6 fusion.94
  238.0 6.7 %fusion.93 = (f32[2,2,256]{2,1,0:T(2,128)S(1)}, bf16[2,2,256,2048]{3,2,1,0:T(8,128)(2,1)}) fusion(pred[256,2048]{1,0:T(8,128)(4,1)S(1)} %fusion.92, bf16[2048,2,96]{0,2,1:T(8,128)(2,1)S(1)} %get-tuple-element.223, bf16[8,256,2,2,96]{1,4,3,2,0:T(8,128)(2,1)} %get-tuple-element.222, s32[]{:T(128)S(6)} %copy.68), kind=kOutput, calls=%fused_computation.97.clone.1 | convolution fusion | flops 415238144 | bytes 6230020 | tf_op jit(solution)/shard_map/while/body/eval_jaxpr/sub | solution.py:85
  244.7 3.6 fusion.94
  251.9 6.7 %fusion.93 = (f32[2,2,256]{2,1,0:T(2,128)S(1)}, bf16[2,2,256,2048]{3,2,1,0:T(8,128)(2,1)}) fusion(pred[256,2048]{1,0:T(8,128)(4,1)S(1)} %fusion.92, bf16[2048,2,96]{0,2,1:T(8,128)(2,1)S(1)} %get-tuple-element.223, bf16[8,256,2,2,96]{1,4,3,2,0:T(8,128)(2,1)} %get-tuple-element.222, s32[]{:T(128)S(6)} %copy.68), kind=kOutput, calls=%fused_computation.97.clone.1 | convolution fusion | flops 415238144 | bytes 6230020 | tf_op jit(solution)/shard_map/while/body/eval_jaxpr/sub | solution.py:85
  258.6 3.6 fusion.94
  263.1 4.6 %convolution_convert_fusion = bf16[1024,1536]{1,0:T(8,128)(2,1)} fusion(bf16[384,1536]{1,0:T(8,128)(2,1)S(1)} %copy-done.14, bf16[2048,384]{1,0:T(8,128)(2,1)} %bitcast.141, s32[]{:T(128)S(6)} %select_n.96), kind=kOutput, calls=%fused_computation.49 | convolution fusion | flops 1209532416 | bytes 5111812 | tf_op jit(solution)/shard_map/dot_general | solution.py:164
  268.0 83.3 %all-reduce = s32[2048]{0:T(1024)S(1)} all-reduce(s32[2048]{0:T(1024)S(1)} %get-tuple-element.128), channel_id=2, replica_groups=mesh['req'=64,'tp'=2] {'req'}, use_global_device_ids=true, to_apply=%add | all-reduce | flops 2048 | bytes 16384
  352.2 17.4 %reshape.234 = bf16[64,1,24576]{2,1,0:T(2,128)(2,1)} reshape(bf16[64,2,12288]{2,1,0:T(2,128)(2,1)} %all-to-all-done) | data formatting | bytes 6291456
  369.6 6.2 %copy.61 = bf16[64,1,24576]{2,0,1:T(8,128)(2,1)S(1)} copy(bf16[64,1,24576]{2,1,0:T(2,128)(2,1)} %reshape.234) | data formatting | bytes 6291456
  375.8 2.7 gather_fusion.1
  378.5 3.2 gather.15
  381.7 4.3 %broadcast_select_fusion.1 = bf16[32,2,2,6144]{3,2,1,0:T(2,128)(2,1)} fusion(pred[32]{0:T(512)(128)(4,1)S(1)} %reduce_or.18, bf16[32,2,2,6144]{3,2,1,0:T(2,128)(2,1)} %gather.15, pred[32]{0:T(512)(128)(4,1)S(1)} %compare_and_fusion.1), kind=kLoop, calls=%fused_computation.55 | loop fusion | flops 1572864 | bytes 3145792 | tf_op jit(solution)/shard_map/jit(_where)/select_n | solution.py:156
  386.1 6.3 %fusion.51 = bf16[1024,1536]{1,0:T(8,128)(2,1)} fusion(bf16[1024,1536]{1,0:T(8,128)(2,1)S(1)} %copy-done.3, bf16[1024,1536]{1,0:T(8,128)(2,1)} %collective-permute-done.1, bf16[384,1536]{1,0:T(8,128)(2,1)} %param.13, bf16[2048,384]{1,0:T(8,128)(2,1)} %bitcast.142, s32[]{:T(128)S(6)} %select_n.95), kind=kOutput, calls=%fused_computation.48 | convolution fusion | flops 1215823872 | bytes 11403268 | tf_op jit(solution)/shard_map/dot_general | solution.py:168
  (130 shorter events, 41.4 us)
Async XLA Ops:
  0.6 18.8 %copy-start = (bf16[1536,768]{1,0:T(8,128)(2,1)S(1)}, bf16[1536,768]{1,0:T(8,128)(2,1)}, u32[]{:S(2)}) copy-start(bf16[1536,768]{1,0:T(8,128)(2,1)} %param.12) | copy-start | bytes 7077892
  0.6 3.7 copy-start.2
  4.3 4.5 %copy-start.8 = (s32[2048]{0:T(1024)S(1)}, s32[2048]{0:T(1024)}, u32[]{:S(2)}) copy-start(s32[2048]{0:T(1024)} %param.9) | copy-start | bytes 24580
  4.4 7.4 %copy-start.15 = (u32[128]{0:T(128)S(1)}, u32[128]{0:T(128)}, u32[]{:S(2)}) copy-start(u32[128]{0:T(128)} %constant.106) | copy-start | bytes 1540
  4.4 8.8 %copy-start.11 = (s32[32]{0:T(128)S(1)}, s32[32]{0:T(128)}, u32[]{:S(2)}) copy-start(s32[32]{0:T(128)} %param.10) | copy-start | bytes 388
  6.8 69.7 %collective-permute-start = (bf16[1024,1536]{1,0:T(8,128)(2,1)}, bf16[1024,1536]{1,0:T(8,128)(2,1)}, u32[]{:S(2)}, u32[]{:S(2)}) collective-permute-start(bf16[1024,1536]{1,0:T(8,128)(2,1)} %fusion.49), channel_id=1, source_target_pairs={{0,1},{1,0},{2,3},{3,2},{4,5},{5,4},{6,7},{7,6},{8,9},{9,8},{10,11... | collective-permute-start | bytes 9437192 | tf_op jit(solution)/shard_map/ppermute | solution.py:120
  101.5 2.4 copy-start.7
  106.7 1.7 copy-start.4
  106.7 1.7 copy-start.5
  106.9 4.6 %copy-start.6 = (bf16[32,64,2,96]{3,2,1,0:T(2,128)(2,1)S(1)}, bf16[32,64,2,96]{3,2,1,0:T(2,128)(2,1)}, u32[]{:S(2)}) copy-start(bf16[32,64,2,96]{3,2,1,0:T(2,128)(2,1)} %convert_element_type.59) | copy-start | bytes 2359300
  121.2 4.4 %copy-start.12 = (pred[64]{0:T(512)(128)(4,1)S(1)}, pred[64]{0:T(512)(128)(4,1)}, u32[]{:S(2)}) copy-start(pred[64]{0:T(512)(128)(4,1)} %fusion.58) | copy-start | bytes 196
  121.2 4.4 %copy-start.13 = (pred[64]{0:T(512)(128)(4,1)S(1)}, pred[64]{0:T(512)(128)(4,1)}, u32[]{:S(2)}) copy-start(pred[64]{0:T(512)(128)(4,1)} %compare_and_fusion) | copy-start | bytes 196
  138.7 13.6 %copy-start.9 = (bf16[2048,192]{0,1:T(8,128)(2,1)S(1)}, bf16[2048,192]{0,1:T(8,128)(2,1)}, u32[]{:S(2)}) copy-start(bf16[2048,192]{0,1:T(8,128)(2,1)} %copy.44) | copy-start | bytes 2359300
  138.7 13.6 %copy-start.10 = (bf16[2048,2,96]{0,2,1:T(8,128)(2,1)S(1)}, bf16[2048,2,96]{0,2,1:T(8,128)(2,1)}, u32[]{:S(2)}) copy-start(bf16[2048,2,96]{0,2,1:T(8,128)(2,1)} %pad_maximum_fusion.3) | copy-start | bytes 2359300
  138.7 213.5 %all-to-all-start = ((bf16[64,2,12288]{2,1,0:T(2,128)(2,1)}), bf16[64,2,12288]{2,1,0:T(2,128)(2,1)}, u32[]{:S(2)}, u32[]{:S(2)}) async-start(bf16[64,2,12288]{2,1,0:T(2,128)(2,1)} %reshape.233), calls=%async_computation | async-start | bytes 6291456 | tf_op jit(solution)/shard_map/all_to_all | solution.py:151
  152.3 110.7 %copy-start.14 = (bf16[384,1536]{1,0:T(8,128)(2,1)S(1)}, bf16[384,1536]{1,0:T(8,128)(2,1)}, u32[]{:S(2)}) copy-start(bf16[384,1536]{1,0:T(8,128)(2,1)} %param.13) | copy-start | bytes 3538948
  267.7 118.4 %collective-permute-start.1 = (bf16[1024,1536]{1,0:T(8,128)(2,1)}, bf16[1024,1536]{1,0:T(8,128)(2,1)}, u32[]{:S(2)}, u32[]{:S(2)}) collective-permute-start(bf16[1024,1536]{1,0:T(8,128)(2,1)} %convolution_convert_fusion), channel_id=1, source_target_pairs={{0,1},{1,0},{2,3},{3,2},{4,5},{5,4},{6,7},{7,6},{8,9},{9,8},{10,11... | collective-permute-start | bytes 9437192 | tf_op jit(solution)/shard_map/ppermute | solution.py:167
  381.7 4.3 %copy-start.3 = (bf16[1024,1536]{1,0:T(8,128)(2,1)S(1)}, bf16[1024,1536]{1,0:T(8,128)(2,1)}, u32[]{:S(2)}) copy-start(bf16[1024,1536]{1,0:T(8,128)(2,1)} %param.8) | copy-start | bytes 9437188
  381.7 10.6 %copy-start.1 = (bf16[1536,768]{1,0:T(8,128)(2,1)S(1)}, bf16[1536,768]{1,0:T(8,128)(2,1)}, u32[]{:S(2)}) copy-start(bf16[1536,768]{1,0:T(8,128)(2,1)} %param.12) | copy-start | bytes 7077892
